TPU v7x, 32 devices: a whole 2x2x4 slice. The times are simulated.
32 devices in a mesh: seq: 16 (over z, x, core), head: 2 (over y).
Axes of the slice: x: 2, y: 2, z: 4, core: 2. Of those that a mesh axis runs over, the one named last changes fastest.
Arguments:
- step_tokens: bfloat16 [2, 12, 8, 2560], P(None, None, None, 'head'), may hold values from -6 to 6
- parents: int32 [2, 12, 8], replicated, may hold values from 0 to 7
- tail_cache: bfloat16 [12, 8, 64, 2048], P(None, 'head', 'seq'), may hold values from -192 to 192
- tail_len: int32 [12], replicated, may hold values from 0 to 62, as said below
- cache: bfloat16 [8, 2048, 2048], P(None, ('seq', 'head')), may hold values from -192 to 192
- cache_len: int32 [8], replicated, may hold values from 256 to 2048, as said below
- prompt_states: bfloat16 [4, 128, 2560], P(None, 'seq', 'head'), may hold values from -6 to 6
- prompt_len: int32 [4], replicated, may hold values from 32 to 128, as said below
- in_gain: float32 [2560], P('head'), may hold values from 0.5 to 1.5
- w_query: bfloat16 [2560, 2048], P('head', 'seq'), may hold values from -0.125 to 0.125
- w_keyval: bfloat16 [2560, 2048], P('head', 'seq'), may hold values from -0.125 to 0.125
- q_gain: float32 [256], replicated, may hold values from 0.6 to 32
- k_gain: float32 [256], replicated, may hold values from 0.6 to 32
- w_out: bfloat16 [2048, 2560], P('seq', 'head'), may hold values from -0.125 to 0.125
- post_gain: float32 [2560], P('head'), may hold values from 0.5 to 1.5
- ffn_gain: float32 [2560], P('head'), may hold values from 0.5 to 1.5
- w_gate: bfloat16 [2560, 10240], P('head', 'seq'), may hold values from -0.125 to 0.125
- w_up: bfloat16 [2560, 10240], P('head', 'seq'), may hold values from -0.125 to 0.125
- w_down: bfloat16 [10240, 2560], P('seq', 'head'), may hold values from -0.0625 to 0.0625
- final_gain: float32 [2560], P('head'), may hold values from 0.5 to 1.5
Outputs:
- decoded: bfloat16 [2, 12, 8, 2560], P(None, None, None, 'head')
Inputs may be any that keep to these rules, and one draw needn't show every extreme that they name: `tail_len`: the first 4 groups have 0; the largest entry is exactly 62. `cache_len`: the largest entry is exactly 2048. `prompt_len`: the largest entry is exactly 128.
All inputs are finite; a program needn't handle non-finite values.
Results may differ from a plain program's by a relative error of at most 0.0055.
The roundings to bfloat16 on the way count: a program that leaves them out, or rounds other values in their place, can miss the bound.
Values may be sent and summed in bfloat16 or wider, within the bound.
No kernel may reach another device: no remote copies, remote signals or barrier semaphores. Data moves between devices by JAX's collectives and lax.ppermute only.
A program may use at most 128 MiB of HBM per device.

v0:
```python
import jax
import jax.numpy as jnp
from jax import lax
from jax.sharding import PartitionSpec as P

D = 2560
QH = 8
KVH = 4
HD = 256
QD = 2048
EPS = 1e-06
NEG = -1e30
QSCALE = 0.0625


def norm_heads(values, gain, scale):
    shaped = values.reshape(values.shape[:-1] + (-1, gain.shape[0]))
    shaped = shaped * lax.rsqrt(jnp.mean(shaped * shaped, -1, keepdims=True) + EPS) * gain * scale
    return shaped.reshape(values.shape)


def finish_keys(pairs, k_gain):
    half = pairs.shape[-1] // 2
    keys = norm_heads(pairs[..., :half], k_gain, 1.0)
    return jnp.concatenate([keys, pairs[..., half:]], -1).astype(jnp.bfloat16)


def split_pairs(pairs):
    half = pairs.shape[-1] // 2
    keys = pairs[..., :half].reshape(pairs.shape[:-1] + (KVH, HD))
    values = pairs[..., half:].reshape(pairs.shape[:-1] + (KVH, HD))
    return (keys, values)


def project_tokens(tokens, in_gain, w_query, w_keyval, q_gain, k_gain):
    flat = tokens.reshape(-1, tokens.shape[-1]).astype(jnp.float32)
    scaled = (flat * in_gain).astype(jnp.bfloat16)
    q_part = jnp.dot(scaled, w_query, preferred_element_type=jnp.float32)
    kv_part = jnp.dot(scaled, w_keyval, preferred_element_type=jnp.float32)
    squares = jnp.sum(flat * flat, -1)
    q_part, kv_part, squares = lax.psum((q_part, kv_part, squares), "head")
    factor = lax.rsqrt(squares / D + EPS)[:, None]
    q_raw = (q_part * factor).astype(jnp.bfloat16)
    kv_raw = (kv_part * factor).astype(jnp.bfloat16)
    q_raw, kv_raw = (
        lax.all_gather(q_raw, "seq", axis=1, tiled=True),
        lax.all_gather(kv_raw, "seq", axis=1, tiled=True),
    )
    queries = norm_heads(q_raw.astype(jnp.float32), q_gain, QSCALE).astype(jnp.bfloat16)
    fresh = finish_keys(kv_raw.astype(jnp.float32), k_gain)
    return (queries, fresh)


def shards(
    step_tokens,
    parents,
    tail_cache,
    tail_len,
    cache,
    cache_len,
    prompt_states,
    prompt_len,
    in_gain,
    w_query,
    w_keyval,
    q_gain,
    k_gain,
    w_out,
    post_gain,
    ffn_gain,
    w_gate,
    w_up,
    w_down,
    final_gain,
):
    f32 = jnp.float32
    bf16 = jnp.bfloat16
    n_head = lax.axis_size("head")
    n_seq = lax.axis_size("seq")
    seq_at = lax.axis_index("seq")
    head_at = lax.axis_index("head")
    flat_at = seq_at * n_head + head_at
    steps, groups, beams, width = step_tokens.shape
    pre = prompt_states.shape[0]
    repeat = QH // KVH
    col_block = QD // n_seq
    block_head = jnp.arange(n_seq) * col_block // HD
    head_pick = (jnp.arange(QH)[:, None] == block_head[None, :]).astype(f32)
    rows = jnp.transpose(prompt_states, (1, 0, 2)).astype(f32)
    prompt_scaled = (rows * in_gain).astype(bf16).reshape(-1, width)
    prompt_squares = jnp.sum(rows * rows, -1).reshape(-1)
    prompt_terms = jnp.dot(
        prompt_scaled,
        lax.all_gather(w_keyval, "seq", axis=1, tiled=True),
        preferred_element_type=f32,
    )
    prompt_sum, prompt_sq = (
        lax.psum_scatter(prompt_terms, "head", scatter_dimension=0, tiled=True),
        lax.psum_scatter(prompt_squares, "head", scatter_dimension=0, tiled=True),
    )
    prompt_pairs = finish_keys(prompt_sum * lax.rsqrt(prompt_sq / D + EPS)[:, None], k_gain)
    prompt_seg = prompt_pairs.shape[0] // pre
    prompt_pairs = jnp.transpose(prompt_pairs.reshape(prompt_seg, pre, -1), (1, 0, 2))
    prompt_keys, prompt_values = split_pairs(prompt_pairs)
    prompt_ok = (flat_at * prompt_seg + jnp.arange(prompt_seg))[None, :] < prompt_len[:, None]
    cache_seg = cache.shape[1]
    cache_keys, cache_values = split_pairs(cache)
    cache_ok = (flat_at * cache_seg + jnp.arange(cache_seg))[None, :] < cache_len[:, None]
    tail_seg = tail_cache.shape[2]
    local_beams = tail_cache.shape[1]
    beam_ids = head_at * local_beams + jnp.arange(local_beams)
    offset = (seq_at * tail_seg + jnp.arange(tail_seg))[None, :] - tail_len[:, None]
    all_beams = jnp.arange(beams)
    every_query, every_fresh = project_tokens(
        step_tokens, in_gain, w_query, w_keyval, q_gain, k_gain
    )
    every_query = every_query.reshape(steps, groups, beams, -1)
    every_fresh = every_fresh.reshape(steps, groups, beams, -1)
    tail_state = tail_cache
    decoded = []
    for step in range(steps):
        query = every_query[step]
        new_pairs = every_fresh[step]
        everyone = lax.all_gather(tail_state, "head", axis=1, tiled=True)
        picks = lax.dynamic_slice_in_dim(parents[step], head_at * local_beams, local_beams, 1)
        tail_state = jnp.take_along_axis(everyone, picks[:, :, None, None], axis=1)
        owner = jnp.broadcast_to(all_beams[None, :, None], (groups, beams, tail_seg))
        mine = lax.dynamic_slice_in_dim(new_pairs, head_at * local_beams, local_beams, 1)
        tail_state = jnp.where((offset == step)[:, None, :, None], mine[:, :, None, :], tail_state)
        tail_ok = (offset <= step)[:, None, None, :] & (
            owner[:, :, None, :] == beam_ids[None, None, :, None]
        )
        shaped = query.reshape(groups, beams, KVH, repeat, HD)
        tail_keys, tail_values = split_pairs(tail_state)
        pre_scores = jnp.einsum(
            "gbkrd,gtkd->gbkrt", shaped[:pre], prompt_keys, preferred_element_type=f32
        )
        dec_scores = jnp.einsum(
            "gbkrd,gtkd->gbkrt", shaped[pre:], cache_keys, preferred_element_type=f32
        )
        tail_scores = jnp.einsum(
            "gbkrd,gctkd->gbkrct", shaped, tail_keys, preferred_element_type=f32
        )
        pre_mask = prompt_ok[:, None, None, None, :]
        dec_mask = cache_ok[:, None, None, None, :]
        tail_mask = tail_ok[:, :, None, None, :, :]
        pre_scores = jnp.where(pre_mask, pre_scores, NEG)
        dec_scores = jnp.where(dec_mask, dec_scores, NEG)
        tail_scores = jnp.where(tail_mask, tail_scores, NEG)
        top = jnp.concatenate([jnp.max(pre_scores, -1), jnp.max(dec_scores, -1)], 0)
        top = jnp.maximum(top, jnp.max(tail_scores, (-2, -1)))
        top = lax.pmax(top, ("seq", "head"))
        pre_weights = jnp.where(pre_mask, jnp.exp(pre_scores - top[:pre, ..., None]), 0.0)
        dec_weights = jnp.where(dec_mask, jnp.exp(dec_scores - top[pre:, ..., None]), 0.0)
        tail_weights = jnp.where(tail_mask, jnp.exp(tail_scores - top[..., None, None]), 0.0)
        total = jnp.concatenate([jnp.sum(pre_weights, -1), jnp.sum(dec_weights, -1)], 0)
        total = total + jnp.sum(tail_weights, (-2, -1))
        weighted = jnp.concatenate(
            [
                jnp.einsum(
                    "gbkrt,gtkd->gbkrd",
                    pre_weights.astype(bf16),
                    prompt_values,
                    preferred_element_type=f32,
                ),
                jnp.einsum(
                    "gbkrt,gtkd->gbkrd",
                    dec_weights.astype(bf16),
                    cache_values,
                    preferred_element_type=f32,
                ),
            ],
            0,
        )
        weighted = weighted + jnp.einsum(
            "gbkrct,gctkd->gbkrd",
            tail_weights.astype(bf16),
            tail_values,
            preferred_element_type=f32,
        )
        weighted = weighted.reshape(groups * beams, -1)
        total = total.reshape(groups * beams, -1)
        spread_total = jnp.sum(total[:, :, None] * head_pick[None, :, :], 1)
        share, own_total = (
            lax.psum_scatter(weighted, "seq", scatter_dimension=1, tiled=True),
            lax.psum_scatter(spread_total, "seq", scatter_dimension=1, tiled=True),
        )
        share, own_total = lax.psum((share, own_total), "head")
        attn = (share / own_total).astype(bf16)
        partial_out = jnp.dot(attn, w_out, preferred_element_type=f32)
        out_proj = lax.psum(partial_out, "seq")
        out_sq = lax.psum(jnp.sum(out_proj * out_proj, -1), "head")
        x_f = step_tokens[step].reshape(groups * beams, -1).astype(f32)
        state = (x_f + out_proj * lax.rsqrt(out_sq / D + EPS)[:, None] * post_gain).astype(bf16)
        state = lax.optimization_barrier(state)
        state_f = state.astype(f32)
        scaled_two = (state_f * ffn_gain).astype(bf16)
        gate_part = jnp.dot(scaled_two, w_gate, preferred_element_type=f32)
        up_part = jnp.dot(scaled_two, w_up, preferred_element_type=f32)
        gate_part, up_part, state_sq = lax.psum(
            (gate_part, up_part, jnp.sum(state_f * state_f, -1)), "head"
        )
        norm_s = lax.rsqrt(state_sq / D + EPS)[:, None]
        inner = (jax.nn.gelu(gate_part * norm_s, approximate=True) * (up_part * norm_s)).astype(
            bf16
        )
        ffn_out = lax.psum(jnp.dot(inner, w_down, preferred_element_type=f32), "seq")
        ffn_sq = lax.psum(jnp.sum(ffn_out * ffn_out, -1), "head")
        result = (state_f + ffn_out * lax.rsqrt(ffn_sq / D + EPS)[:, None] * final_gain).astype(
            bf16
        )
        decoded.append(result.reshape(groups, beams, -1))
    return jnp.stack(decoded)


def solution(mesh):
    return jax.shard_map(
        shards,
        mesh=mesh,
        in_specs=(
            P(None, None, None, "head"),
            P(),
            P(None, "head", "seq", None),
            P(),
            P(None, ("seq", "head"), None),
            P(),
            P(None, "seq", "head"),
            P(),
            P("head"),
            P("head", "seq"),
            P("head", "seq"),
            P(),
            P(),
            P("seq", "head"),
            P("head"),
            P("head"),
            P("head", "seq"),
            P("head", "seq"),
            P("seq", "head"),
            P("head"),
        ),
        out_specs=P(None, None, None, "head"),
        check_vma=False,
    )
```

profile of v0, /device:TPU:0, one launch (start us, length us, event | category | flops | bytes accessed | tf_op | source)
XLA Modules:
  0.0 628.8 jit_solution(9408125753058318404)
XLA Ops:
  7.9 1.9 fusion.145
  12.6 5.8 all-reduce.11
  19.1 17.0 %all-reduce.28.cloned.1.call-done = (f32[192,128]{1,0:T(8,128)}, f32[192,128]{1,0:T(8,128)}) async-done(((f32[192,128]{1,0:T(8,128)}, f32[192,128]{1,0:T(8,128)}), (f32[192,128]{1,0:T(8,128)}, f32[192,128]{1,0:T(8,128)})) %all-reduce.28.cloned.1.call-update) | async-done | bytes 196624 | tf_op jit(solution)/shard_map/psum | solution.py:41
  37.1 23.5 %all_gather.17 = bf16[192,2048]{1,0:T(8,128)(2,1)S(1)} all-gather(bf16[192,128]{1,0:T(8,128)(2,1)S(1)} %get-tuple-element.70), channel_id=1, replica_groups=mesh['seq'=16,'head'=2] {'seq'}, dimensions={1}, use_global_device_ids=true | all-gather | bytes 835584 | tf_op jit(solution)/shard_map/all_gather | solution.py:47
  66.4 2.9 gather_fusion
  73.5 2.7 fusion.131
  77.9 1.9 reshape.375
  83.1 22.2 %all_gather.16 = bf16[192,2048]{1,0:T(8,128)(2,1)S(1)} all-gather(bf16[192,128]{1,0:T(8,128)(2,1)S(1)} %get-tuple-element.71), channel_id=1, replica_groups=mesh['seq'=16,'head'=2] {'seq'}, dimensions={1}, use_global_device_ids=true | all-gather | bytes 835584 | tf_op jit(solution)/shard_map/all_gather | solution.py:46
  105.5 1.8 copy.246
  107.2 2.4 reduce_sum.180
  121.2 2.0 fusion.37
  124.3 4.0 gather_fusion.1
  128.3 1.9 select_select_fusion
  130.2 28.0 %all-gather.4.cloned.1.call-done = bf16[1280,2048]{1,0:T(8,128)(2,1)} async-done(((bf16[1280,128]{1,0:T(8,128)(2,1)}), bf16[1280,2048]{1,0:T(8,128)(2,1)}) %all-gather.4.cloned.1.call-update) | async-done | bytes 5242896 | tf_op jit(solution)/shard_map/all_gather | solution.py:94
  158.2 4.2 fusion.143
  164.5 2.1 fusion.34
  167.7 4.7 reduce-scatter.4.cloned.1.call-done
  173.9 1.9 fusion.142
  175.9 1.9 fusion.140
  177.9 40.8 %all-reduce.3 = (f32[12,8,4,2]{1,3,2,0:T(2,128)S(1)}, f32[12,8,4,2]{1,3,2,0:T(2,128)S(1)}) all-reduce(f32[12,8,4,2]{1,3,2,0:T(2,128)S(1)} %maximum_maximum_fusion.1, f32[12,8,4,2]{1,3,2,0:T(2,128)S(1)} %maximum_maximum_fusion), channel_id=1, replica_groups=mesh['seq'=16,'head'=2] {'seq','head'}, use_global_device_ids=true, to_apply=%region_35.37 | all-reduce | flops 1536 | bytes 12288 | tf_op jit(solution)/shard_map/pmax | solution.py:152
  235.1 60.1 %all-reduce.4 = (f32[96,16]{0,1:T(8,128)S(1)}, f32[96,16]{0,1:T(8,128)S(1)}) all-reduce(f32[96,16]{0,1:T(8,128)S(1)} %get-tuple-element.7, f32[96,16]{0,1:T(8,128)S(1)} %get-tuple-element.6), channel_id=7, replica_groups=mesh['seq'=16,'head'=2] {'seq'}, use_global_device_ids=true, to_apply=%region_42.44.clone | all-reduce | flops 3072 | bytes 24576
  297.6 45.9 %reduce-scatter.8.cloned.1.call-done = f32[96,128]{1,0:T(8,128)} async-done(((f32[96,2048]{1,0:T(8,128)}), f32[96,128]{1,0:T(8,128)}) %reduce-scatter.8.cloned.1.call-update) | async-done | bytes 49168 | tf_op jit(solution)/shard_map/reduce_scatter | solution.py:185
  343.6 22.5 %all-reduce.24.cloned.1.call-done = (f32[96,128]{1,0:T(8,128)}, f32[96]{0:T(128)}, f32[96,128]{1,0:T(8,128)}, f32[96]{0:T(128)}) async-done(((f32[96,128]{1,0:T(8,128)}, f32[96]{0:T(128)}, f32[96,128]{1,0:T(8,128)}, f32[96]{0:T(128)}), (f32[96,128]{1,0:T(8,128)}, f32[96]{0:T(128)}, f32[96,128]{1,0:T(8,128)}, f32[96]{0:T(128)})) %all-reduce.24.cloned.1.call-update) | async-done | bytes 99088 | tf_op jit(solution)/shard_map/psum | solution.py:188
  366.1 1.9 fusion.111
  367.9 1.9 fusion.110
  369.9 94.0 %all-reduce.22.cloned.1.call-done = (f32[96,1280]{1,0:T(8,128)}, f32[96,1280]{1,0:T(8,128)}) async-done(((f32[96,1280]{1,0:T(8,128)}, f32[96,1280]{1,0:T(8,128)}), (f32[96,1280]{1,0:T(8,128)}, f32[96,1280]{1,0:T(8,128)})) %all-reduce.22.cloned.1.call-update) | async-done | bytes 983056 | tf_op jit(solution)/shard_map/psum | solution.py:191
  466.2 4.9 all-reduce.9
  477.7 4.9 all-reduce.8
  482.7 33.1 %all-reduce.26.cloned.1.call-done = (f32[96,640]{1,0:T(8,128)}, f32[96,640]{1,0:T(8,128)}, f32[96,640]{1,0:T(8,128)}, f32[96,640]{1,0:T(8,128)}) async-done(((f32[96,640]{1,0:T(8,128)}, f32[96,640]{1,0:T(8,128)}, f32[96,640]{1,0:T(8,128)}, f32[96,640]{1,0:T(8,128)}), (f32[96,640]{1,0:T(8,128)}, f32[96,640]{1,0:T(8,128)}, f32[96,640]{1,0:T(8,128)}, f32[96,640]{1,0:T(8,128)})) %all-reduce.26.cloned.1.call-update) | async-done | bytes 983056 | tf_op jit(solution)/shard_map/psum | solution.py:200
  515.7 2.4 fusion.81
  519.5 93.3 %all-reduce.20.cloned.1.call-done = (f32[96,1280]{1,0:T(8,128)}, f32[96,1280]{1,0:T(8,128)}) async-done(((f32[96,1280]{1,0:T(8,128)}, f32[96,1280]{1,0:T(8,128)}), (f32[96,1280]{1,0:T(8,128)}, f32[96,1280]{1,0:T(8,128)})) %all-reduce.20.cloned.1.call-update) | async-done | bytes 983056 | tf_op jit(solution)/shard_map/psum | solution.py:207
  615.1 4.9 all-reduce.7
  (274 shorter events, 70.4 us)
Async XLA Ops:
  6.5 509.2 %copy-start = (bf16[640,1280]{1,0:T(8,128)(2,1)S(1)}, bf16[640,1280]{1,0:T(8,128)(2,1)}, u32[]{:S(2)}) copy-start(bf16[640,1280]{1,0:T(8,128)(2,1)} %param.40) | copy-start | bytes 4915204
  6.5 29.6 %all-reduce.28.cloned.1.call-start = ((), (), s32[]{:S(2)}) async-start(), calls=%async_computation.13 | async-start | bytes 393216 | tf_op jit(solution)/shard_map/psum | solution.py:41
  7.9 10.6 %copy-start.47 = (s32[12]{0:T(128)S(1)}, s32[12]{0:T(128)}, u32[]{:S(2)}) copy-start(s32[12]{0:T(128)} %param.25) | copy-start | bytes 148
  10.8 55.7 %all-gather.6.cloned.1.call-start = ((), (), s32[]{:S(2)}) async-start(), calls=%async_computation.5 | async-start | bytes 2359296 | tf_op jit(solution)/shard_map/all_gather | solution.py:124
  11.5 112.7 %all-gather.8.cloned.1.call-start = ((), (), s32[]{:S(2)}) async-start(), calls=%async_computation.7 | async-start | bytes 2359296 | tf_op jit(solution)/shard_map/all_gather | solution.py:124
  11.8 52.8 %copy-start.32 = (f32[1,2,4,128]{3,1,2,0:T(2,128)}, f32[1,2,4,128]{3,1,2,0:T(2,128)S(1)}, u32[]{:S(2)}) copy-start(f32[1,2,4,128]{3,1,2,0:T(2,128)S(1)} %copy.245) | copy-start | bytes 12292
  71.1 87.1 %all-gather.4.cloned.1.call-start = ((), (), s32[]{:S(2)}) async-start(), calls=%async_computation.3 | async-start | bytes 5570560 | tf_op jit(solution)/shard_map/all_gather | solution.py:94
  71.6 100.7 %reduce-scatter.4.cloned.1.call-start = ((), (), s32[]{:S(2)}) async-start(), calls=%async_computation.4 | async-start | bytes 393216 | tf_op jit(solution)/shard_map/reduce_scatter | solution.py:98
  76.3 5.4 copy-start.50
  76.3 6.1 copy-start.49
  82.4 33.9 %copy-start.35 = (pred[8,64]{1,0:T(8,128)(4,1)}, pred[8,64]{1,0:T(8,128)(4,1)S(1)}, u32[]{:S(2)}) copy-start(pred[8,64]{1,0:T(8,128)(4,1)S(1)} %broadcast_compare_fusion) | copy-start | bytes 1540
  83.1 41.0 %copy-start.24 = (pred[12,8,4,4]{0,1,3,2:T(8,128)(4,1)}, pred[12,8,4,4]{0,1,3,2:T(8,128)(4,1)S(1)}, u32[]{:S(2)}) copy-start(pred[12,8,4,4]{0,1,3,2:T(8,128)(4,1)S(1)} %get-tuple-element.72) | copy-start | bytes 4612
  123.2 5.0 copy-start.15
  123.2 5.0 copy-start.39
  124.3 33.9 %copy-start.17 = (bf16[32,1280]{1,0:T(8,128)(2,1)S(1)}, bf16[32,1280]{1,0:T(8,128)(2,1)}, u32[]{:S(2)}) copy-start(bf16[32,1280]{1,0:T(8,128)(2,1)} %reshape.371) | copy-start | bytes 245764
  162.4 135.2 %reduce-scatter.6.cloned.1.call-start = ((), (), s32[]{:S(2)}) async-start(), calls=%async_computation.6 | async-start | bytes 835584 | tf_op jit(solution)/shard_map/reduce_scatter | solution.py:185
  164.5 7.9 %copy-start.46 = (f32[16]{0:T(128)S(1)}, f32[16]{0:T(128)}, u32[]{:S(2)}) copy-start(f32[16]{0:T(128)} %fusion.118) | copy-start | bytes 196
  166.6 7.1 %copy-start.33 = (f32[1,2,4,128]{3,1,2,0:T(2,128)S(1)}, f32[1,2,4,128]{3,1,2,0:T(2,128)}, u32[]{:S(2)}) copy-start(f32[1,2,4,128]{3,1,2,0:T(2,128)} %copy-done.32) | copy-start | bytes 12292
  167.5 6.4 %copy-start.42 = (pred[4,4]{1,0:T(4,128)(4,1)S(1)}, pred[4,4]{1,0:T(4,128)(4,1)}, u32[]{:S(2)}) copy-start(pred[4,4]{1,0:T(4,128)(4,1)} %broadcast_compare_fusion.1) | copy-start | bytes 52
  167.5 10.3 %copy-start.29 = (f32[8,8,4,2]{1,3,2,0:T(2,128)S(1)}, f32[8,8,4,2]{1,3,2,0:T(2,128)}, u32[]{:S(2)}) copy-start(f32[8,8,4,2]{1,3,2,0:T(2,128)} %get-tuple-element.78) | copy-start | bytes 6148
  167.5 10.4 %copy-start.28 = (f32[8,8,4,2]{1,3,2,0:T(2,128)S(1)}, f32[8,8,4,2]{1,3,2,0:T(2,128)}, u32[]{:S(2)}) copy-start(f32[8,8,4,2]{1,3,2,0:T(2,128)} %get-tuple-element.74) | copy-start | bytes 6148
  173.8 50.0 %copy-start.12 = (f32[8,8,4,2,64]{4,1,3,2,0:T(8,128)S(1)}, f32[8,8,4,2,64]{4,1,3,2,0:T(8,128)}, u32[]{:S(2)}) copy-start(f32[8,8,4,2,64]{4,1,3,2,0:T(8,128)} %get-tuple-element.79) | copy-start | bytes 393220
  226.8 116.6 %reduce-scatter.8.cloned.1.call-start = ((), (), s32[]{:S(2)}) async-start(), calls=%async_computation.8 | async-start | bytes 835584 | tf_op jit(solution)/shard_map/reduce_scatter | solution.py:185
  233.1 133.0 %copy-start.10 = (bf16[128,1280]{1,0:T(8,128)(2,1)S(1)}, bf16[128,1280]{1,0:T(8,128)(2,1)}, u32[]{:S(2)}) copy-start(bf16[128,1280]{1,0:T(8,128)(2,1)} %param.35) | copy-start | bytes 983044
  233.1 133.0 %all-reduce.24.cloned.1.call-start = ((), (), s32[]{:S(2)}) async-start(), calls=%async_computation.11 | async-start | bytes 198656 | tf_op jit(solution)/shard_map/psum | solution.py:188
  343.5 120.4 %all-reduce.22.cloned.1.call-start = ((), (), s32[]{:S(2)}) async-start(), calls=%async_computation.10 | async-start | bytes 1966080 | tf_op jit(solution)/shard_map/psum | solution.py:191
  367.9 103.3 %copy-start.37 = (f32[1280]{0:T(1024)S(1)}, f32[1280]{0:T(1024)}, u32[]{:S(2)}) copy-start(f32[1280]{0:T(1024)} %param.36) | copy-start | bytes 15364
  369.8 103.1 %copy-start.2 = (bf16[1280,640]{1,0:T(8,128)(2,1)S(1)}, bf16[1280,640]{1,0:T(8,128)(2,1)}, u32[]{:S(2)}) copy-start(bf16[1280,640]{1,0:T(8,128)(2,1)} %param.39) | copy-start | bytes 4915204
  369.8 103.1 %copy-start.26 = (f32[1280]{0:T(1024)S(1)}, f32[1280]{0:T(1024)}, u32[]{:S(2)}) copy-start(f32[1280]{0:T(1024)} %param.37) | copy-start | bytes 15364
  369.9 145.9 %all-reduce.26.cloned.1.call-start = ((), (), s32[]{:S(2)}) async-start(), calls=%async_computation.12 | async-start | bytes 1966080 | tf_op jit(solution)/shard_map/psum | solution.py:200
  477.4 135.4 %all-reduce.20.cloned.1.call-start = ((), (), s32[]{:S(2)}) async-start(), calls=%async_computation.9 | async-start | bytes 1966080 | tf_op jit(solution)/shard_map/psum | solution.py:207
  519.4 100.6 %copy-start.38 = (f32[1280]{0:T(1024)S(1)}, f32[1280]{0:T(1024)}, u32[]{:S(2)}) copy-start(f32[1280]{0:T(1024)} %param.41) | copy-start | bytes 15364
  (32 other events, 88.4 us)
Sparse Core Ops, SparseCore 0:
  10.9 25.1 all-reduce.27
  37.6 27.1 all-gather.5
  71.2 25.6 all-gather.7
  98.9 59.2 all-gather.3
  162.5 9.8 reduce-scatter.3
  227.0 57.3 reduce-scatter.5
  287.9 55.5 reduce-scatter.7
  346.1 19.9 all-reduce.23
  370.0 93.8 all-reduce.21
  477.5 38.1 all-reduce.25
  519.6 93.1 all-reduce.19
where the time goes:
time: 630 us; the launch traced here: 629 us
  waiting for transfers between devices  340 us (54%)
  blocking collectives  167 us (27%)
  local copies, waits for them, and re-layouts  40.9 us (6%)
  matrix products  38.3 us (6%)
  other arithmetic  27.2 us (4%)
  between operations  14.9 us (2%)
    psum x1, waiting for transfers between devices, shards(): out_proj = lax.psum(partial_out, 'seq')  94 us
    psum x1, waiting for transfers between devices, shards(): lax.psum(jnp.dot(inner, w_down, preferred_element_type=f32), 'seq')  93.3 us
    unnamed x1, blocking collectives  60.1 us
    reduce_scatter x2, waiting for transfers between devices, shards(): lax.psum_scatter(weighted, 'seq', scatter_dimension=1, tiled=True)  45.9 us
    pmax x1, blocking collectives, shards(): top = lax.pmax(top, ('seq', 'head'))  40.8 us
    psum x1, waiting for transfers between devices, shards(): lax.psum((gate_part, up_part, jnp.sum(state_f * state_f, -1)), 'head')  33.1 us
    all_gather x1, waiting for transfers between devices, shards(): lax.all_gather(w_keyval, 'seq', axis=1, tiled=True)  28 us
    all_gather x1, blocking collectives, project_tokens(): lax.all_gather(kv_raw, 'seq', axis=1, tiled=True)  23.5 us
  transfers between devices with their start and end apart: 11, of which 8 were waited for; matrix products, arithmetic and copies ran while one was open for 9% of the time, Pallas kernels for 0%

commit v1 on v0

--- a/solution.py
+++ b/solution.py
@@ -11,6 +11,28 @@
 EPS = 1e-06
 NEG = -1e30
 QSCALE = 0.0625
+
+
+def try_all_slices(field_in, at_axis):
+    upper = list(field_in.shape[1:])
+    upper[at_axis] *= field_in.shape[0]
+    tall = jnp.moveaxis(field_in, 0, at_axis).reshape(upper)
+    return tall
+
+
+def pack_wall_in(arr, peer_axis):
+    even, z_new = (lax.axis_size(peer_axis), lax.axis_index(peer_axis))
+    block_next, t_next = (arr[None], 1)
+    while t_next < even:
+        y_new = lax.ppermute(
+            block_next, peer_axis, list(map(lambda dev_i: (dev_i, dev_i ^ t_next), range(even)))
+        )
+        block_out = z_new & t_next == 0
+        block_next = jnp.concatenate(
+            [jnp.where(block_out, block_next, y_new), jnp.where(block_out, y_new, block_next)]
+        )
+        t_next *= 2
+    return block_next
 
 
 def norm_heads(values, gain, scale):
@@ -42,8 +64,13 @@
     factor = lax.rsqrt(squares / D + EPS)[:, None]
     q_raw = (q_part * factor).astype(jnp.bfloat16)
     kv_raw = (kv_part * factor).astype(jnp.bfloat16)
+
+    def track_pipes(chunk, inner_x, d_out):
+        h_now = try_all_slices(pack_wall_in(chunk, inner_x), d_out)
+        return h_now
+
     q_raw, kv_raw = (
-        lax.all_gather(q_raw, "seq", axis=1, tiled=True),
+        track_pipes(q_raw, "seq", 1),
         lax.all_gather(kv_raw, "seq", axis=1, tiled=True),
     )
     queries = norm_heads(q_raw.astype(jnp.float32), q_gain, QSCALE).astype(jnp.bfloat16)

time: 630 us -> 630 us (level)
  blocking collectives: 167 us -> 145 us
  waiting for transfers between devices: 340 us -> 361 us
    all_gather x1 -> x0, blocking collectives: 22.2 us -> none  [project_tokens(): lax.all_gather(q_raw, 'seq', axis=1, tiled=True)]
    ppermute x0 -> x4, waiting for transfers between devices: none -> 18 us  [pack_wall_in(): lax.ppermute(block_next, peer_axis, list(map(lambda dev_i: (dev_i, dev_i...]
  transfers between devices with their start and end apart: 11 -> 15, of which waited for: 8 -> 12; matrix products, arithmetic and copies ran while one was open for 9% -> 9% of each run, Pallas kernels for 0% -> 0%
where the time goes in v1:
time: 630 us; the launch traced here: 629 us
  waiting for transfers between devices  361 us (57%)
  blocking collectives  145 us (23%)
  local copies, waits for them, and re-layouts  40.8 us (6%)
  matrix products  38.1 us (6%)
  other arithmetic  25.6 us (4%)
  between operations  15 us (2%)
    psum x1, waiting for transfers between devices, shards(): out_proj = lax.psum(partial_out, 'seq')  94 us
    psum x1, waiting for transfers between devices, shards(): lax.psum(jnp.dot(inner, w_down, preferred_element_type=f32), 'seq')  93.3 us
    unnamed x1, blocking collectives  60 us
    reduce_scatter x2, waiting for transfers between devices, shards(): lax.psum_scatter(weighted, 'seq', scatter_dimension=1, tiled=True)  46 us
    pmax x1, blocking collectives, shards(): top = lax.pmax(top, ('seq', 'head'))  40.8 us
    psum x1, waiting for transfers between devices, shards(): lax.psum((gate_part, up_part, jnp.sum(state_f * state_f, -1)), 'head')  33.1 us
    all_gather x1, waiting for transfers between devices, shards(): lax.all_gather(w_keyval, 'seq', axis=1, tiled=True)  31.3 us
    all_gather x1, blocking collectives, project_tokens(): lax.all_gather(kv_raw, 'seq', axis=1, tiled=True)  23.5 us
  transfers between devices with their start and end apart: 15, of which 12 were waited for; matrix products, arithmetic and copies ran while one was open for 9% of the time, Pallas kernels for 0%

profile of v1, /device:TPU:0, one launch (start us, length us, event | category | flops | bytes accessed | tf_op | source)
XLA Modules:
  0.0 628.7 jit_solution(13528066797220769758)
XLA Ops:
  7.9 1.9 fusion.147
  13.1 5.8 all-reduce.11
  19.6 16.5 %all-reduce.28.cloned.1.call-done = (f32[192,128]{1,0:T(8,128)}, f32[192,128]{1,0:T(8,128)}) async-done(((f32[192,128]{1,0:T(8,128)}, f32[192,128]{1,0:T(8,128)}), (f32[192,128]{1,0:T(8,128)}, f32[192,128]{1,0:T(8,128)})) %all-reduce.28.cloned.1.call-update) | async-done | bytes 196624 | tf_op jit(solution)/shard_map/psum | solution.py:63
  37.1 23.5 %all_gather.13 = bf16[192,2048]{1,0:T(8,128)(2,1)S(1)} all-gather(bf16[192,128]{1,0:T(8,128)(2,1)S(1)} %get-tuple-element.78), channel_id=1, replica_groups=mesh['seq'=16,'head'=2] {'seq'}, dimensions={1}, use_global_device_ids=true | all-gather | bytes 835584 | tf_op jit(solution)/shard_map/all_gather | solution.py:74
  65.7 2.9 gather_fusion
  71.5 2.8 fusion.133
  76.3 4.4 collective-permute-done.1
  81.8 5.3 collective-permute-done.2
  94.7 1.9 reshape.380
  99.2 7.4 %collective-permute-done.3 = bf16[8,192,128]{2,1,0:T(8,128)(2,1)} collective-permute-done((bf16[8,192,128]{2,1,0:T(8,128)(2,1)S(1)}, bf16[8,192,128]{2,1,0:T(8,128)(2,1)}, u32[]{:S(2)}, u32[]{:S(2)}) %collective-permute-start.3) | collective-permute-done | bytes 393248 | tf_op jit(solution)/shard_map/ppermute | solution.py:27
  118.1 2.0 fusion.38
  121.1 4.0 gather_fusion.1
  125.1 1.8 select_select_fusion
  126.9 31.3 %all-gather.4.cloned.1.call-done = bf16[1280,2048]{1,0:T(8,128)(2,1)} async-done(((bf16[1280,128]{1,0:T(8,128)(2,1)}), bf16[1280,2048]{1,0:T(8,128)(2,1)}) %all-gather.4.cloned.1.call-update) | async-done | bytes 5242896 | tf_op jit(solution)/shard_map/all_gather | solution.py:121
  158.2 4.2 fusion.145
  164.6 2.1 fusion.35
  167.7 4.8 reduce-scatter.4.cloned.1.call-done
  174.0 1.9 fusion.144
  175.9 1.9 fusion.142
  178.0 40.8 %all-reduce.3 = (f32[12,8,4,2]{1,3,2,0:T(2,128)S(1)}, f32[12,8,4,2]{1,3,2,0:T(2,128)S(1)}) all-reduce(f32[12,8,4,2]{1,3,2,0:T(2,128)S(1)} %maximum_maximum_fusion.1, f32[12,8,4,2]{1,3,2,0:T(2,128)S(1)} %maximum_maximum_fusion), channel_id=1, replica_groups=mesh['seq'=16,'head'=2] {'seq','head'}, use_global_device_ids=true, to_apply=%region_36.38 | all-reduce | flops 1536 | bytes 12288 | tf_op jit(solution)/shard_map/pmax | solution.py:179
  235.1 60.0 %all-reduce.4 = (f32[96,16]{0,1:T(8,128)S(1)}, f32[96,16]{0,1:T(8,128)S(1)}) all-reduce(f32[96,16]{0,1:T(8,128)S(1)} %get-tuple-element.7, f32[96,16]{0,1:T(8,128)S(1)} %get-tuple-element.6), channel_id=7, replica_groups=mesh['seq'=16,'head'=2] {'seq'}, use_global_device_ids=true, to_apply=%region_43.45.clone | all-reduce | flops 3072 | bytes 24576
  297.4 46.0 %reduce-scatter.8.cloned.1.call-done = f32[96,128]{1,0:T(8,128)} async-done(((f32[96,2048]{1,0:T(8,128)}), f32[96,128]{1,0:T(8,128)}) %reduce-scatter.8.cloned.1.call-update) | async-done | bytes 49168 | tf_op jit(solution)/shard_map/reduce_scatter | solution.py:212
  343.5 22.5 %all-reduce.24.cloned.1.call-done = (f32[96,128]{1,0:T(8,128)}, f32[96]{0:T(128)}, f32[96,128]{1,0:T(8,128)}, f32[96]{0:T(128)}) async-done(((f32[96,128]{1,0:T(8,128)}, f32[96]{0:T(128)}, f32[96,128]{1,0:T(8,128)}, f32[96]{0:T(128)}), (f32[96,128]{1,0:T(8,128)}, f32[96]{0:T(128)}, f32[96,128]{1,0:T(8,128)}, f32[96]{0:T(128)})) %all-reduce.24.cloned.1.call-update) | async-done | bytes 99088 | tf_op jit(solution)/shard_map/psum | solution.py:215
  366.0 1.9 fusion.113
  367.8 1.9 fusion.112
  369.8 94.0 %all-reduce.22.cloned.1.call-done = (f32[96,1280]{1,0:T(8,128)}, f32[96,1280]{1,0:T(8,128)}) async-done(((f32[96,1280]{1,0:T(8,128)}, f32[96,1280]{1,0:T(8,128)}), (f32[96,1280]{1,0:T(8,128)}, f32[96,1280]{1,0:T(8,128)})) %all-reduce.22.cloned.1.call-update) | async-done | bytes 983056 | tf_op jit(solution)/shard_map/psum | solution.py:218
  466.1 4.9 all-reduce.9
  477.6 4.9 all-reduce.8
  482.6 33.1 %all-reduce.26.cloned.1.call-done = (f32[96,640]{1,0:T(8,128)}, f32[96,640]{1,0:T(8,128)}, f32[96,640]{1,0:T(8,128)}, f32[96,640]{1,0:T(8,128)}) async-done(((f32[96,640]{1,0:T(8,128)}, f32[96,640]{1,0:T(8,128)}, f32[96,640]{1,0:T(8,128)}, f32[96,640]{1,0:T(8,128)}), (f32[96,640]{1,0:T(8,128)}, f32[96,640]{1,0:T(8,128)}, f32[96,640]{1,0:T(8,128)}, f32[96,640]{1,0:T(8,128)})) %all-reduce.26.cloned.1.call-update) | async-done | bytes 983056 | tf_op jit(solution)/shard_map/psum | solution.py:227
  515.6 2.4 fusion.82
  519.4 93.3 %all-reduce.20.cloned.1.call-done = (f32[96,1280]{1,0:T(8,128)}, f32[96,1280]{1,0:T(8,128)}) async-done(((f32[96,1280]{1,0:T(8,128)}, f32[96,1280]{1,0:T(8,128)}), (f32[96,1280]{1,0:T(8,128)}, f32[96,1280]{1,0:T(8,128)})) %all-reduce.20.cloned.1.call-update) | async-done | bytes 983056 | tf_op jit(solution)/shard_map/psum | solution.py:234
  615.0 4.9 all-reduce.7
  (289 shorter events, 76.6 us)
Async XLA Ops:
  6.5 509.1 %copy-start = (bf16[640,1280]{1,0:T(8,128)(2,1)S(1)}, bf16[640,1280]{1,0:T(8,128)(2,1)}, u32[]{:S(2)}) copy-start(bf16[640,1280]{1,0:T(8,128)(2,1)} %param.40) | copy-start | bytes 4915204
  6.5 29.6 %all-reduce.28.cloned.1.call-start = ((), (), s32[]{:S(2)}) async-start(), calls=%async_computation.13 | async-start | bytes 393216 | tf_op jit(solution)/shard_map/psum | solution.py:63
  7.9 11.1 %copy-start.48 = (s32[12]{0:T(128)S(1)}, s32[12]{0:T(128)}, u32[]{:S(2)}) copy-start(s32[12]{0:T(128)} %param.25) | copy-start | bytes 148
  10.8 54.9 %all-gather.6.cloned.1.call-start = ((), (), s32[]{:S(2)}) async-start(), calls=%async_computation.5 | async-start | bytes 2359296 | tf_op jit(solution)/shard_map/all_gather | solution.py:151
  11.5 109.6 %all-gather.8.cloned.1.call-start = ((), (), s32[]{:S(2)}) async-start(), calls=%async_computation.7 | async-start | bytes 2359296 | tf_op jit(solution)/shard_map/all_gather | solution.py:151
  11.8 52.8 %copy-start.33 = (f32[1,2,4,128]{3,1,2,0:T(2,128)}, f32[1,2,4,128]{3,1,2,0:T(2,128)S(1)}, u32[]{:S(2)}) copy-start(f32[1,2,4,128]{3,1,2,0:T(2,128)S(1)} %copy.282) | copy-start | bytes 12292
  70.3 87.9 %all-gather.4.cloned.1.call-start = ((), (), s32[]{:S(2)}) async-start(), calls=%async_computation.3 | async-start | bytes 5570560 | tf_op jit(solution)/shard_map/all_gather | solution.py:121
  70.9 101.6 %reduce-scatter.4.cloned.1.call-start = ((), (), s32[]{:S(2)}) async-start(), calls=%async_computation.4 | async-start | bytes 393216 | tf_op jit(solution)/shard_map/reduce_scatter | solution.py:125
  71.5 49.4 %copy-start.25 = (pred[12,8,4,4]{0,1,3,2:T(8,128)(4,1)}, pred[12,8,4,4]{0,1,3,2:T(8,128)(4,1)S(1)}, u32[]{:S(2)}) copy-start(pred[12,8,4,4]{0,1,3,2:T(8,128)(4,1)S(1)} %get-tuple-element.80) | copy-start | bytes 4612
  71.5 96.0 %copy-start.23 = (pred[12,8,4,4]{0,1,3,2:T(8,128)(4,1)}, pred[12,8,4,4]{0,1,3,2:T(8,128)(4,1)S(1)}, u32[]{:S(2)}) copy-start(pred[12,8,4,4]{0,1,3,2:T(8,128)(4,1)S(1)} %get-tuple-element.81) | copy-start | bytes 4612
  71.5 9.8 %copy-start.51 = (s32[4]{0:T(128)S(1)}, s32[4]{0:T(128)}, u32[]{:S(2)}) copy-start(s32[4]{0:T(128)} %param.29) | copy-start | bytes 52
  74.3 1.2 collective-permute-start
  74.7 38.4 %copy-start.36 = (pred[8,64]{1,0:T(8,128)(4,1)}, pred[8,64]{1,0:T(8,128)(4,1)S(1)}, u32[]{:S(2)}) copy-start(pred[8,64]{1,0:T(8,128)(4,1)S(1)} %broadcast_compare_fusion) | copy-start | bytes 1540
  75.6 5.1 collective-permute-start.1
  80.7 6.4 %collective-permute-start.2 = (bf16[4,192,128]{2,1,0:T(8,128)(2,1)S(1)}, bf16[4,192,128]{2,1,0:T(8,128)(2,1)S(1)}, u32[]{:S(2)}, u32[]{:S(2)}) collective-permute-start(bf16[4,192,128]{2,1,0:T(8,128)(2,1)S(1)} %pad_maximum_fusion.4), channel_id=1, source_target_pairs={{0,8},{2,10},{4,12},{6,14},{8,0},{10,2},{12,4},{14,6},{16,24},{18,... | collective-permute-start | bytes 589832 | tf_op jit(solution)/shard_map/ppermute | solution.py:27
  87.9 18.8 %collective-permute-start.3 = (bf16[8,192,128]{2,1,0:T(8,128)(2,1)S(1)}, bf16[8,192,128]{2,1,0:T(8,128)(2,1)}, u32[]{:S(2)}, u32[]{:S(2)}) collective-permute-start(bf16[8,192,128]{2,1,0:T(8,128)(2,1)S(1)} %pad_maximum_fusion.3), channel_id=1, source_target_pairs={{0,16},{2,18},{4,20},{6,22},{8,24},{10,26},{12,28},{14,30},{16,0},... | collective-permute-start | bytes 1179656 | tf_op jit(solution)/shard_map/ppermute | solution.py:27
  121.1 37.2 %copy-start.18 = (bf16[32,1280]{1,0:T(8,128)(2,1)S(1)}, bf16[32,1280]{1,0:T(8,128)(2,1)}, u32[]{:S(2)}) copy-start(bf16[32,1280]{1,0:T(8,128)(2,1)} %reshape.376) | copy-start | bytes 245764
  162.5 134.9 %reduce-scatter.6.cloned.1.call-start = ((), (), s32[]{:S(2)}) async-start(), calls=%async_computation.6 | async-start | bytes 835584 | tf_op jit(solution)/shard_map/reduce_scatter | solution.py:212
  164.6 7.9 %copy-start.47 = (f32[16]{0:T(128)S(1)}, f32[16]{0:T(128)}, u32[]{:S(2)}) copy-start(f32[16]{0:T(128)} %fusion.120) | copy-start | bytes 196
  167.5 10.4 %copy-start.30 = (f32[8,8,4,2]{1,3,2,0:T(2,128)S(1)}, f32[8,8,4,2]{1,3,2,0:T(2,128)}, u32[]{:S(2)}) copy-start(f32[8,8,4,2]{1,3,2,0:T(2,128)} %get-tuple-element.86) | copy-start | bytes 6148
  167.5 10.4 %copy-start.29 = (f32[8,8,4,2]{1,3,2,0:T(2,128)S(1)}, f32[8,8,4,2]{1,3,2,0:T(2,128)}, u32[]{:S(2)}) copy-start(f32[8,8,4,2]{1,3,2,0:T(2,128)} %get-tuple-element.82) | copy-start | bytes 6148
  173.9 50.0 %copy-start.14 = (f32[8,8,4,2,64]{4,1,3,2,0:T(8,128)S(1)}, f32[8,8,4,2,64]{4,1,3,2,0:T(8,128)}, u32[]{:S(2)}) copy-start(f32[8,8,4,2,64]{4,1,3,2,0:T(8,128)} %get-tuple-element.87) | copy-start | bytes 393220
  226.9 116.5 %reduce-scatter.8.cloned.1.call-start = ((), (), s32[]{:S(2)}) async-start(), calls=%async_computation.8 | async-start | bytes 835584 | tf_op jit(solution)/shard_map/reduce_scatter | solution.py:212
  233.0 133.0 %copy-start.12 = (bf16[128,1280]{1,0:T(8,128)(2,1)S(1)}, bf16[128,1280]{1,0:T(8,128)(2,1)}, u32[]{:S(2)}) copy-start(bf16[128,1280]{1,0:T(8,128)(2,1)} %param.35) | copy-start | bytes 983044
  233.0 132.9 %all-reduce.24.cloned.1.call-start = ((), (), s32[]{:S(2)}) async-start(), calls=%async_computation.11 | async-start | bytes 198656 | tf_op jit(solution)/shard_map/psum | solution.py:215
  343.4 120.4 %all-reduce.22.cloned.1.call-start = ((), (), s32[]{:S(2)}) async-start(), calls=%async_computation.10 | async-start | bytes 1966080 | tf_op jit(solution)/shard_map/psum | solution.py:218
  367.8 103.3 %copy-start.38 = (f32[1280]{0:T(1024)S(1)}, f32[1280]{0:T(1024)}, u32[]{:S(2)}) copy-start(f32[1280]{0:T(1024)} %param.36) | copy-start | bytes 15364
  369.7 103.1 %copy-start.2 = (bf16[1280,640]{1,0:T(8,128)(2,1)S(1)}, bf16[1280,640]{1,0:T(8,128)(2,1)}, u32[]{:S(2)}) copy-start(bf16[1280,640]{1,0:T(8,128)(2,1)} %param.39) | copy-start | bytes 4915204
  369.7 103.1 %copy-start.27 = (f32[1280]{0:T(1024)S(1)}, f32[1280]{0:T(1024)}, u32[]{:S(2)}) copy-start(f32[1280]{0:T(1024)} %param.37) | copy-start | bytes 15364
  369.8 145.9 %all-reduce.26.cloned.1.call-start = ((), (), s32[]{:S(2)}) async-start(), calls=%async_computation.12 | async-start | bytes 1966080 | tf_op jit(solution)/shard_map/psum | solution.py:227
  477.3 135.4 %all-reduce.20.cloned.1.call-start = ((), (), s32[]{:S(2)}) async-start(), calls=%async_computation.9 | async-start | bytes 1966080 | tf_op jit(solution)/shard_map/psum | solution.py:234
  519.4 100.6 %copy-start.39 = (f32[1280]{0:T(1024)S(1)}, f32[1280]{0:T(1024)}, u32[]{:S(2)}) copy-start(f32[1280]{0:T(1024)} %param.41) | copy-start | bytes 15364
  (37 other events, 112.7 us)
Sparse Core Ops, SparseCore 0:
  10.9 25.1 all-reduce.27
  37.7 27.1 all-gather.5
  70.5 26.4 all-gather.7
  99.0 59.2 all-gather.3
  162.6 9.8 reduce-scatter.3
  227.0 57.3 reduce-scatter.5
  287.9 55.4 reduce-scatter.7
  346.0 19.9 all-reduce.23
  369.9 93.8 all-reduce.21
  477.4 38.1 all-reduce.25
  519.5 93.1 all-reduce.19
